TPU v7x, 256 devices: a whole 4x4x8 slice. The times are simulated.
256 devices in a mesh: req: 32 (over x, z), kv: 8 (over y, core).
Axes of the slice: x: 4, y: 4, z: 8, core: 2. Of those that a mesh axis runs over, the one named last changes fastest.
Arguments:
- states: bfloat16 [256, 2560], P(('req', 'kv')), may hold values from -6 to 6
- norm_gain: bfloat16 [2560], replicated, may hold values from 0.099609375 to 1.8984375
- w_query: bfloat16 [2560, 2560], P(None, 'kv'), may hold values from -0.125 to 0.125
- key_projection_weight: bfloat16 [2560, 640], P(None, 'kv'), may hold values from -0.125 to 0.125
- value_projection_weight: bfloat16 [2560, 640], P(None, 'kv'), may hold values from -0.125 to 0.125
- cache_keys: bfloat16 [256, 8, 80, 4096], P('req', 'kv')
- value_cache_slots: bfloat16 [256, 8, 80, 4096], P('req', 'kv'), may hold values from -6 to 6
- lengths: int32 [256], P('req'), may hold values from 1 to 16383, as said below
- write_pos: int32 [256], P('req'), may hold values from 0 to 4095, as said below
- dealing: int32 [256], replicated, may hold values from 0 to 255, each once
Outputs:
- context: bfloat16 [256, 2560], P(('req', 'kv'))
Inputs may be any that keep to these rules, and one draw needn't show every extreme that they name: `lengths`: largest value is reached by some request in every draw. write_pos equals lengths modulo 4096. `dealing`: A permutation of the requests.
All inputs are finite; a program needn't handle non-finite values.
Results may differ from a plain program's by a relative error of at most 0.022.
The roundings to bfloat16 on the way count: a program that leaves them out, or rounds other values in their place, can miss the bound.
Values may be sent and summed in bfloat16 or wider, within the bound.
No kernel may reach another device: no remote copies, remote signals or barrier semaphores. Data moves between devices by JAX's collectives and lax.ppermute only.
A program may use at most 64 MiB of HBM per device.

v0:
```python
import jax
import jax.numpy as jnp
from jax import lax
from jax.sharding import PartitionSpec as P

HEAD_DIMENSION = 80


def apply_rotary(tensor, positions):
    half_width = tensor.shape[-1] // 2
    frequency = 10000.0 ** (-(jnp.arange(half_width, dtype=jnp.float32) * 2.0 / tensor.shape[-1]))
    angles = positions.astype(jnp.float32)[:, None] * frequency[None, :]
    cosine = jnp.cos(angles)[:, None, :]
    sine_part = jnp.sin(angles)[:, None, :]
    front_half = tensor[..., :half_width]
    back_half = tensor[..., half_width:]
    return jnp.concatenate(
        [front_half * cosine - back_half * sine_part, back_half * cosine + front_half * sine_part],
        axis=-1,
    )


def local(
    states,
    norm_gain,
    w_query,
    key_projection_weight,
    value_projection_weight,
    cache_keys,
    value_cache_slots,
    lengths,
    write_pos,
    dealing,
):
    kv_count = lax.axis_size("kv")
    per_device = states.shape[0]
    group_rows = per_device * kv_count
    group_index = lax.axis_index("req")
    kv_index = lax.axis_index("kv")
    total_rows = dealing.shape[0]
    dealt_ids = lax.dynamic_slice_in_dim(dealing, group_index * group_rows, group_rows)
    all_rows = lax.all_gather(states, ("req", "kv"), axis=0, tiled=True)
    dealt_rows = jnp.take(all_rows, dealt_ids, axis=0)
    wide_rows = dealt_rows.astype(jnp.float32)
    inv_rms = lax.rsqrt(jnp.mean(wide_rows * wide_rows, axis=1, keepdims=True) + 1e-05)
    normalized_input = (wide_rows * inv_rms * norm_gain.astype(jnp.float32)[None, :]).astype(
        jnp.bfloat16
    )
    head_size = HEAD_DIMENSION
    heads_dev = key_projection_weight.shape[1] // head_size
    queries_per_group = w_query.shape[1] // key_projection_weight.shape[1]
    window_size = cache_keys.shape[3]
    query_vectors = jnp.dot(normalized_input, w_query, preferred_element_type=jnp.float32).reshape(
        group_rows, heads_dev * queries_per_group, head_size
    )
    query_vectors = (
        apply_rotary(query_vectors, lengths)
        .astype(jnp.bfloat16)
        .reshape(group_rows, heads_dev, queries_per_group, head_size)
    )
    fresh_key_rows = jnp.dot(
        normalized_input, key_projection_weight, preferred_element_type=jnp.float32
    ).reshape(group_rows, heads_dev, head_size)
    fresh_key_rows = apply_rotary(fresh_key_rows, lengths).astype(jnp.bfloat16)
    fresh_value_rows = (
        jnp.dot(normalized_input, value_projection_weight, preferred_element_type=jnp.float32)
        .astype(jnp.bfloat16)
        .reshape(group_rows, heads_dev, head_size)
    )
    score_scale = 1.0 / head_size**0.5
    scores = (
        jnp.einsum("rkgh,rkhw->rkgw", query_vectors, cache_keys, preferred_element_type=jnp.float32)
        * score_scale
    )
    own_score = (
        jnp.einsum(
            "rkgh,rkh->rkg", query_vectors, fresh_key_rows, preferred_element_type=jnp.float32
        )
        * score_scale
    )
    slot_ids = lax.broadcasted_iota(jnp.int32, (group_rows, 1, 1, window_size), 3)
    at_write = slot_ids == write_pos[:, None, None, None]
    scores = jnp.where(at_write, own_score[..., None], scores)
    scores = jnp.where(slot_ids <= lengths[:, None, None, None], scores, -jnp.inf)
    row_max = jnp.max(scores, axis=-1, keepdims=True)
    expd = jnp.exp(scores - row_max)
    softmax_weights = (expd / jnp.sum(expd, axis=-1, keepdims=True)).astype(jnp.bfloat16)
    stale_weights = jnp.where(at_write, jnp.zeros((), jnp.bfloat16), softmax_weights)
    fresh_weight = jnp.sum(
        jnp.where(at_write, softmax_weights, jnp.zeros((), jnp.bfloat16)).astype(jnp.float32),
        axis=-1,
    )
    mixed = jnp.einsum(
        "rkgw,rkhw->rkgh", stale_weights, value_cache_slots, preferred_element_type=jnp.float32
    )
    mixed = mixed + fresh_weight[..., None] * fresh_value_rows[:, :, None, :].astype(jnp.float32)
    attended = mixed.reshape(group_rows, heads_dev * queries_per_group * head_size).astype(
        jnp.bfloat16
    )
    inverse = jnp.zeros((total_rows,), jnp.int32).at[dealing].set(jnp.arange(total_rows))
    request_rows = lax.all_to_all(attended, "kv", split_axis=0, concat_axis=1, tiled=True)
    all_context = lax.all_gather(request_rows, ("req", "kv"), axis=0, tiled=True)
    own_ids = lax.dynamic_slice_in_dim(
        inverse, (group_index * kv_count + kv_index) * per_device, per_device
    )
    result = jnp.take(all_context, own_ids, axis=0)
    return result


def solution(mesh):
    in_specs = (
        P(("req", "kv"), None),
        P(),
        P(None, "kv"),
        P(None, "kv"),
        P(None, "kv"),
        P("req", "kv", None, None),
        P("req", "kv", None, None),
        P("req"),
        P("req"),
        P(),
    )
    out_specs = P(("req", "kv"), None)
    return jax.shard_map(local, mesh=mesh, in_specs=in_specs, out_specs=out_specs, check_vma=False)
```

profile of v0, /device:TPU:1, one launch (start us, length us, event | category | flops | bytes accessed | tf_op | source)
XLA Modules:
  0.0 256.5 jit_solution(114267257454325564)
XLA Ops:
  6.5 0.0 copy-start
  6.5 0.0 all-gather.5.cloned.1.call-start
  6.5 0.7 all-gather.5.cloned.1.call-update
  7.3 0.0 all-gather.7.cloned.1.call-start
  7.3 0.7 convert_element_type.52
  8.0 0.7 convert_element_type.50
  8.7 0.8 compare_and_fusion
  9.4 0.1 multiply_cosine_fusion.1
  9.6 0.8 iota_compare_fusion
  10.3 109.8 %all-gather.5.cloned.1.call-done = bf16[256,1,2560]{2,1,0:T(2,128)(2,1)} async-done(((bf16[1,1,2560]{2,1,0:T(2,128)(2,1)}), bf16[256,1,2560]{2,1,0:T(2,128)(2,1)}) %all-gather.5.cloned.1.call-update) | async-done | bytes 1310736 | tf_op jit(solution)/shard_map/all_gather | solution.py:42
  120.1 1.9 copy.19
  122.0 0.6 gather_fusion
  122.6 0.2 fusion.26
  122.8 1.3 convolution_bitcast_fusion
  124.1 0.1 fusion.41
  124.2 1.3 fusion.22
  125.5 0.0 copy-done
  125.5 0.5 fusion.47
  126.0 0.1 reshape.261
  126.1 0.1 maximum_bitcast_fusion
  126.2 0.1 subtract_convert_fusion
  126.3 0.2 fusion.38
  126.5 0.0 copy-start.1
  126.5 3.7 %fusion.49 = (f32[8,4]{1,0:T(8,128)S(1)}, f32[8,4,4096]{2,1,0:T(4,128)S(1)}) fusion(bf16[8,1,80,4096]{3,2,1,0:T(8,128)(2,1)} %param.15, f32[8,4]{1,0:T(8,128)S(1)} %broadcast_multiply_fusion, pred[8,4096]{1,0:T(8,128)(4,1)S(1)} %get-tuple-element.28, pred[8,4096]{1,0:T(8,128)(4,1)S(1)} %get-tuple-element.29, bf16[8,4,40]{2,1,0:T(4,128)(2,1)S(1)} %get-tuple-element.21, ...), kind=kOutput, calls=%fused_computation.64 | convolution fusion | flops 21641216 | bytes 5838080 | tf_op jit(solution)/shard_map/sub | solution.py:86
  130.2 0.4 convert_reduce_fusion
  130.5 3.9 %fusion.19 = bf16[8,4,80]{2,1,0:T(4,128)(2,1)S(1)} fusion(bf16[8,1,80,4096]{3,2,1,0:T(8,128)(2,1)} %param.16, bf16[8,4,4096]{2,1,0:T(4,128)(2,1)S(1)} %get-tuple-element.17, pred[8,4096]{1,0:T(8,128)(4,1)S(1)} %get-tuple-element.29, f32[8,80]{1,0:T(8,128)S(1)} %fusion.22, f32[8,4]{1,0:T(8,128)S(1)} %get-tuple-element.16), kind=kOutput, calls=%fused_computation.14 | convolution fusion | flops 21110272 | bytes 5545600 | tf_op jit(solution)/shard_map/rkgw,rkhw->rkgh/dot_general | solution.py:93
  134.5 0.1 convert_element_type.59
  134.6 0.5 broadcast.209
  135.1 0.7 reduce.7
  135.8 0.1 reshape.323
  135.9 8.8 %all_to_all.13 = bf16[8,2,160]{2,1,0:T(2,128)(2,1)S(1)} all-to-all(bf16[8,2,160]{2,1,0:T(2,128)(2,1)S(1)} %reshape.323), channel_id=1, replica_groups=mesh['req'=32,'kv'=8] {'kv'}, dimensions={0} | all-to-all | bytes 10240 | tf_op jit(solution)/shard_map/all_to_all | solution.py:101
  144.7 0.1 reshape.324
  144.9 0.7 reshape.311
  145.5 0.0 all-gather.7.cloned.1.call-update
  145.6 0.0 copy-done.1
  145.6 1.4 scatter_custom_fusion
  147.0 0.7 dynamic_slice.6
  149.6 98.7 %all-gather.7.cloned.1.call-done = bf16[256,1,2560]{2,1,0:T(2,128)(2,1)} async-done(((bf16[1,1,2560]{2,1,0:T(2,128)(2,1)}), bf16[256,1,2560]{2,1,0:T(2,128)(2,1)}) %all-gather.7.cloned.1.call-update) | async-done | bytes 1310736 | tf_op jit(solution)/shard_map/all_gather | solution.py:102
  248.3 1.3 fusion.29
  (7 shorter events, 0.1 us)
Async XLA Ops:
  6.5 119.0 %copy-start = (bf16[2560,320]{0,1:T(8,128)(2,1)S(1)}, bf16[2560,320]{0,1:T(8,128)(2,1)}, u32[]{:S(2)}) copy-start(bf16[2560,320]{0,1:T(8,128)(2,1)} %param.12) | copy-start | bytes 4915204
  6.5 113.6 %all-gather.5.cloned.1.call-start = ((), (), s32[]{:S(2)}) async-start(), calls=%async_computation.1 | async-start | bytes 2631680 | tf_op jit(solution)/shard_map/all_gather | solution.py:42
  7.3 241.1 %all-gather.7.cloned.1.call-start = ((), (), s32[]{:S(2)}) async-start(), calls=%async_computation.2 | async-start | bytes 2631680 | tf_op jit(solution)/shard_map/all_gather | solution.py:102
  126.5 19.1 %copy-start.1 = (s32[256]{0:T(256)S(1)}, s32[256]{0:T(256)}, u32[]{:S(2)}) copy-start(s32[256]{0:T(256)} %param.19) | copy-start | bytes 3076
Sparse Core Ops, SparseCore 0:
  11.0 109.0 all-gather.4
  145.7 102.5 all-gather.6
where the time goes:
time: 257 us; the launch traced here: 256 us
  waiting for transfers between devices  209 us (81%)
  between operations  15.4 us (6%)
  matrix products  10.9 us (4%)
  blocking collectives  8.83 us (3%)
  local copies, waits for them, and re-layouts  6.11 us (2%)
  other arithmetic  5.97 us (2%)
    all_gather x1, waiting for transfers between devices, local(): all_rows = lax.all_gather(states, ('req', 'kv'), axis=0, tiled=True)  110 us
    all_gather x1, waiting for transfers between devices, local(): lax.all_gather(request_rows, ('req', 'kv'), axis=0, tiled=True)  98.7 us
    all_to_all x1, blocking collectives, local(): lax.all_to_all(attended, 'kv', split_axis=0, concat_axis=1, tiled=True)  8.83 us
  transfers between devices with their start and end apart: 2, of which 2 were waited for; matrix products, arithmetic and copies ran while one was open for 2% of the time, Pallas kernels for 0%

commit v1 on v0

--- a/solution.py
+++ b/solution.py
@@ -4,6 +4,15 @@
 from jax.sharding import PartitionSpec as P
 
 HEAD_DIMENSION = 80
+take_skins = lambda named_axis, z: jnp.concatenate(
+    lax.all_to_all(
+        jnp.stack(jnp.split(z, lax.axis_size(named_axis), axis=0)),
+        axis_name=named_axis,
+        split_axis=0,
+        concat_axis=0,
+    ),
+    axis=1,
+)
 
 
 def apply_rotary(tensor, positions):
@@ -98,7 +107,7 @@
         jnp.bfloat16
     )
     inverse = jnp.zeros((total_rows,), jnp.int32).at[dealing].set(jnp.arange(total_rows))
-    request_rows = lax.all_to_all(attended, "kv", split_axis=0, concat_axis=1, tiled=True)
+    request_rows = take_skins("kv", attended)
     all_context = lax.all_gather(request_rows, ("req", "kv"), axis=0, tiled=True)
     own_ids = lax.dynamic_slice_in_dim(
         inverse, (group_index * kv_count + kv_index) * per_device, per_device

time: 257 us -> 258 us (level)
  no operation moved by 1% of the time
where the time goes in v1:
time: 258 us; the launch traced here: 257 us
  waiting for transfers between devices  209 us (81%)
  between operations  15.4 us (6%)
  matrix products  10.9 us (4%)
  blocking collectives  8.83 us (3%)
  local copies, waits for them, and re-layouts  6.79 us (3%)
  other arithmetic  5.97 us (2%)
    all_gather x1, waiting for transfers between devices, local(): all_rows = lax.all_gather(states, ('req', 'kv'), axis=0, tiled=True)  110 us
    all_gather x1, waiting for transfers between devices, local(): lax.all_gather(request_rows, ('req', 'kv'), axis=0, tiled=True)  98.7 us
    all_to_all x1, blocking collectives, lax.all_to_all(jnp.stack(jnp.split(z, lax.axis_size(named_axis), axis=0))...  8.83 us
  transfers between devices with their start and end apart: 2, of which 2 were waited for; matrix products, arithmetic and copies ran while one was open for 2% of the time, Pallas kernels for 0%

profile of v1, /device:TPU:1, one launch (start us, length us, event | category | flops | bytes accessed | tf_op | source)
XLA Modules:
  0.0 257.2 jit_solution(3858385671227756299)
XLA Ops:
  6.5 0.0 copy-start
  6.5 0.0 all-gather.5.cloned.1.call-start
  6.5 0.7 all-gather.5.cloned.1.call-update
  7.3 0.0 all-gather.7.cloned.1.call-start
  7.3 0.7 convert_element_type.43
  8.0 0.7 convert_element_type.41
  8.7 0.8 compare_and_fusion
  9.4 0.1 multiply_cosine_fusion.1
  9.6 0.8 iota_compare_fusion
  10.3 109.8 %all-gather.5.cloned.1.call-done = bf16[256,1,2560]{2,1,0:T(2,128)(2,1)} async-done(((bf16[1,1,2560]{2,1,0:T(2,128)(2,1)}), bf16[256,1,2560]{2,1,0:T(2,128)(2,1)}) %all-gather.5.cloned.1.call-update) | async-done | bytes 1310736 | tf_op jit(solution)/shard_map/all_gather | solution.py:51
  120.1 1.9 copy.25
  122.0 0.6 gather_fusion
  122.6 0.2 fusion.26
  122.8 1.3 convolution_bitcast_fusion
  124.1 0.1 fusion.41
  124.2 1.3 fusion.22
  125.5 0.0 copy-done
  125.5 0.5 fusion.47
  126.0 0.1 reshape.264
  126.1 0.1 maximum_bitcast_fusion
  126.2 0.1 subtract_convert_fusion
  126.3 0.2 fusion.38
  126.5 0.0 copy-start.1
  126.5 3.7 %fusion.50 = (f32[8,4]{1,0:T(8,128)S(1)}, f32[8,4,4096]{2,1,0:T(4,128)S(1)}) fusion(bf16[8,1,80,4096]{3,2,1,0:T(8,128)(2,1)} %param.15, f32[8,4]{1,0:T(8,128)S(1)} %broadcast_multiply_fusion, pred[8,4096]{1,0:T(8,128)(4,1)S(1)} %get-tuple-element.36, pred[8,4096]{1,0:T(8,128)(4,1)S(1)} %get-tuple-element.37, bf16[8,4,40]{2,1,0:T(4,128)(2,1)S(1)} %get-tuple-element.21, ...), kind=kOutput, calls=%fused_computation.73 | convolution fusion | flops 21641216 | bytes 5838080 | tf_op jit(solution)/shard_map/sub | solution.py:95
  130.2 0.4 convert_reduce_fusion
  130.6 4.0 %fusion.19 = bf16[8,4,80]{2,1,0:T(4,128)(2,1)S(1)} fusion(bf16[8,1,80,4096]{3,2,1,0:T(8,128)(2,1)} %param.16, bf16[8,4,4096]{2,1,0:T(4,128)(2,1)S(1)} %get-tuple-element.17, pred[8,4096]{1,0:T(8,128)(4,1)S(1)} %get-tuple-element.37, f32[8,80]{1,0:T(8,128)S(1)} %fusion.22, f32[8,4]{1,0:T(8,128)S(1)} %get-tuple-element.16), kind=kOutput, calls=%fused_computation.14 | convolution fusion | flops 21110272 | bytes 5545600 | tf_op jit(solution)/shard_map/rkgw,rkhw->rkgh/dot_general | solution.py:102
  134.5 0.1 stack.34
  134.6 0.1 stack.33
  134.7 0.1 stack.32
  134.8 0.1 stack.31
  134.9 0.1 stack.30
  135.0 0.1 stack.29
  135.1 0.1 stack.28
  135.1 0.1 stack.27
  135.3 0.5 broadcast.209
  135.9 0.7 reduce.7
  136.5 0.1 reshape.327
  136.6 8.8 %all_to_all.5 = bf16[8,2,160]{2,1,0:T(2,128)(2,1)S(1)} all-to-all(bf16[8,2,160]{2,1,0:T(2,128)(2,1)S(1)} %reshape.327), channel_id=1, replica_groups=mesh['req'=32,'kv'=8] {'kv'}, dimensions={0} | all-to-all | bytes 10240 | tf_op jit(solution)/shard_map/all_to_all | solution.py:8
  145.5 0.1 reshape.328
  145.6 0.7 reshape.315
  146.3 0.0 all-gather.7.cloned.1.call-update
  146.3 0.0 copy-done.1
  146.3 1.4 scatter_custom_fusion
  147.7 0.7 dynamic_slice.6
  150.3 98.7 %all-gather.7.cloned.1.call-done = bf16[256,1,2560]{2,1,0:T(2,128)(2,1)} async-done(((bf16[1,1,2560]{2,1,0:T(2,128)(2,1)}), bf16[256,1,2560]{2,1,0:T(2,128)(2,1)}) %all-gather.7.cloned.1.call-update) | async-done | bytes 1310736 | tf_op jit(solution)/shard_map/all_gather | solution.py:111
  249.0 1.3 fusion.29
  (16 shorter events, 0.2 us)
Async XLA Ops:
  6.5 119.0 %copy-start = (bf16[2560,320]{0,1:T(8,128)(2,1)S(1)}, bf16[2560,320]{0,1:T(8,128)(2,1)}, u32[]{:S(2)}) copy-start(bf16[2560,320]{0,1:T(8,128)(2,1)} %param.12) | copy-start | bytes 4915204
  6.5 113.6 %all-gather.5.cloned.1.call-start = ((), (), s32[]{:S(2)}) async-start(), calls=%async_computation.1 | async-start | bytes 2631680 | tf_op jit(solution)/shard_map/all_gather | solution.py:51
  7.3 241.8 %all-gather.7.cloned.1.call-start = ((), (), s32[]{:S(2)}) async-start(), calls=%async_computation.2 | async-start | bytes 2631680 | tf_op jit(solution)/shard_map/all_gather | solution.py:111
  126.5 19.8 %copy-start.1 = (s32[256]{0:T(256)S(1)}, s32[256]{0:T(256)}, u32[]{:S(2)}) copy-start(s32[256]{0:T(256)} %param.19) | copy-start | bytes 3076
Sparse Core Ops, SparseCore 0:
  11.0 109.0 all-gather.4
  146.4 102.5 all-gather.6
